TPU v7x, 512 devices: a whole 4x8x8 slice. The times are simulated.
512 devices in a mesh: seq: 16 (over z, y_lo), wt: 32 (over x, y_hi, core).
Axes of the slice: x: 4, y: 8 (y_hi: 4, y_lo: 2; y = y_hi * 2 + y_lo), z: 8, core: 2. Of those that a mesh axis runs over, the one named last changes fastest.
Arguments:
- tokens_in: bfloat16 [3584, 4608], P('seq', 'wt'), may hold values from -6 to 6
- norm_gain: float32 [4608], P('wt'), may hold values from 0.25 to 1.75
- positions: int32 [3584], P('seq'), may hold values from 0 to 2687, as said below
- blocks: bfloat16 [32, 64, 128, 128], P('wt'), may hold values from -0.125 to 0.125
- slot_code: int32 [32, 64], P('wt'), may hold values from -1 to 2303, as said below
- out_grad: bfloat16 [3584, 4096], P('seq', 'wt'), may hold values from -6 to 6
Outputs:
- attn_out: bfloat16 [3584, 4096], P('seq', 'wt')
- tokens_grad: bfloat16 [3584, 4608], P('seq', 'wt')
- gain_grad: float32 [4608], P('wt')
- block_grads: bfloat16 [32, 64, 128, 128], P('wt')
Inputs may be any that keep to these rules, and one draw needn't show every extreme that they name: Positions count the tokens of each document from 0: positions[0] = 0 and every later entry is either 0 (a new document starts) or the entry before plus one. The longest document has exactly 2688 tokens. slot_code[o, s] is -1 for an empty slot, else u * 2 * 36 + p with head u and 0 <= p < 72; no value other than -1 appears twice. One owner holds at most 2 blocks for one head; in every draw some owner holds 2 blocks for every head and some head has 2 blocks at every owner.
All inputs are finite; a program needn't handle non-finite values.
Results may differ from a plain program's by a relative error of at most 0.023.
Values may be sent and summed in bfloat16 or wider, within the bound.
No kernel may reach another device: no remote copies, remote signals or barrier semaphores. Data moves between devices by JAX's collectives and lax.ppermute only.
A program may use at most 64 MiB of HBM per device.

v0:
```python
import jax
import jax.numpy as jnp
from jax import lax
from jax.sharding import PartitionSpec as P

D = 4608
HD = 128
BLK = 128
CAP = 2
query_scale = 144.0 ** (-0.5)
soft_cap = 50.0
norm_eps = 1e-06


def from_partner(block, axis, stride):
    count = lax.axis_size(axis)
    route = []
    for low in range(count):
        high = low | 1 << stride
        if high != low and high < count:
            route += [(low, high), (high, low)]
    return lax.ppermute(block, axis, route)


def shifted(value, axis, steps):
    count = lax.axis_size(axis)
    initial, last = (max(0, -steps), min(count, count - steps))
    return lax.ppermute(value, axis, [(source, source + steps) for source in range(initial, last)])


def rope_tables(positions, head_width):
    half_width = head_width // 2
    frequency = 10000.0 ** (-2.0 * jnp.arange(half_width, dtype=jnp.float32) / head_width)
    angles = positions.astype(jnp.float32)[:, None] * frequency[None, :]
    return (jnp.cos(angles), jnp.sin(angles))


def rotate(vector, cos_table, sin_table):
    half_width = vector.shape[-1] // 2
    first_half = vector[..., :half_width]
    second_half = vector[..., half_width:]
    return jnp.concatenate(
        [
            first_half * cos_table - second_half * sin_table,
            first_half * sin_table + second_half * cos_table,
        ],
        axis=-1,
    )


def contract(left, right):
    return lax.dot_general(
        left, right, (((1,), (1,)), ((), ())), preferred_element_type=jnp.float32
    )


def contract_rows(left, right):
    return lax.dot_general(
        left, right, (((0,), (0,)), ((), ())), preferred_element_type=jnp.float32
    )


def body(tokens_in, norm_gain, positions, blocks, slot_code, out_grad):
    tok_rows = tokens_in.shape[0]
    feat = tokens_in.shape[1]
    groups = lax.axis_size("wt")
    slab_index = lax.axis_index("seq")
    is_even = lax.axis_index("wt") % 2 == 0
    pos_count = 2 * (D // BLK)
    row_blocks = pos_count // 2
    slot_codes = slot_code[0]
    is_live = slot_codes >= 0
    target_user = jnp.where(is_live, slot_codes // pos_count, 0)
    user_match = (
        (target_user[:, None] == jnp.arange(groups, dtype=jnp.int32)[None, :]) & is_live[:, None]
    ).astype(jnp.int32)
    earlier = jnp.cumsum(user_match, axis=0) - user_match
    slot_rank = jnp.sum(earlier * user_match, axis=1)
    dump_slot = groups * CAP
    slot_dest = jnp.where(is_live, target_user * CAP + slot_rank, dump_slot)
    block_place = (slot_codes - target_user * pos_count).astype(jnp.float32)
    outgoing = jnp.zeros((dump_slot + 1, BLK, BLK), jnp.bfloat16).at[slot_dest].set(blocks[0])
    outgoing_pos = (
        jnp.full((dump_slot + 1,), -1.0, jnp.float32)
        .at[slot_dest]
        .set(block_place)
        .astype(jnp.bfloat16)
    )
    arrived, arrived_pos = (
        lax.all_to_all(
            outgoing[:dump_slot].reshape(groups, CAP, BLK, BLK),
            "wt",
            split_axis=0,
            concat_axis=0,
            tiled=True,
        ),
        lax.all_to_all(
            outgoing_pos[:dump_slot].reshape(groups, CAP),
            "wt",
            split_axis=0,
            concat_axis=0,
            tiled=True,
        ),
    )
    gain_hi = lax.reduce_precision(norm_gain, exponent_bits=8, mantissa_bits=7)
    gain_rest = norm_gain - gain_hi
    gain_mid = lax.reduce_precision(gain_rest, exponent_bits=8, mantissa_bits=7)
    gain_lo = gain_rest - gain_mid
    gain_rows = jnp.stack([gain_hi, gain_mid, gain_lo]).astype(jnp.bfloat16)
    side_rows = 8
    gathered = lax.all_gather(
        jnp.concatenate(
            [tokens_in, gain_rows, jnp.zeros((side_rows - 3, feat), jnp.bfloat16)], axis=0
        ),
        "wt",
        axis=1,
        tiled=True,
    )
    tokens_full = gathered[:tok_rows]
    gain_parts = gathered[tok_rows : tok_rows + 3].astype(jnp.float32)
    gain_full = gain_parts[0] + gain_parts[1] + gain_parts[2]
    full_f32 = tokens_full.astype(jnp.float32)
    squares = jnp.sum(full_f32 * full_f32, axis=1)
    inv_rms = lax.rsqrt(squares / D + norm_eps)
    scaled_full = full_f32 * inv_rms[:, None]
    gained_full = scaled_full * gain_full[None, :]
    normed = gained_full.astype(jnp.bfloat16)
    scaled = tokens_in.astype(jnp.float32) * inv_rms[:, None]
    arrival = arrived_pos.reshape(-1).astype(jnp.int32)
    arrival = jnp.where(arrival < 0, pos_count, arrival)
    weight_table = (
        jnp.zeros((pos_count + 1, BLK, BLK), jnp.bfloat16)
        .at[arrival]
        .set(arrived.reshape(-1, BLK, BLK))
    )
    w_query = weight_table[:row_blocks].reshape(D, HD)
    w_pair = weight_table[row_blocks:pos_count].reshape(D, HD)
    query_proj = jnp.dot(normed, w_query, preferred_element_type=jnp.float32)
    pair_proj = jnp.dot(normed, w_pair, preferred_element_type=jnp.float32)
    cos_table, sin_table = rope_tables(positions, HD)
    query_rot = (rotate(query_proj, cos_table, sin_table) * query_scale).astype(jnp.bfloat16)
    own_pair = jnp.where(is_even, rotate(pair_proj, cos_table, sin_table), pair_proj).astype(
        jnp.bfloat16
    )
    partner = from_partner(own_pair, "wt", 0)
    key_rows = jnp.where(is_even, own_pair, partner)
    value_rows = jnp.where(is_even, partner, own_pair)
    reach_slabs = lax.axis_size("seq") // 2
    window = reach_slabs * tok_rows
    key_value = jnp.concatenate([key_rows, value_rows], axis=1)
    key_list = [key_rows]
    value_list = [value_rows]
    for offset in range(1, reach_slabs + 1):
        prev = shifted(key_value, "seq", offset)
        key_list.append(prev[:, :HD])
        value_list.append(prev[:, HD:])
    key_all = jnp.concatenate(key_list, axis=0)
    value_all = jnp.concatenate(value_list, axis=0)
    local_index = jnp.arange(tok_rows, dtype=jnp.int32)
    query_index = slab_index * tok_rows + local_index
    key_index = jnp.concatenate(
        [(slab_index - offset) * tok_rows + local_index for offset in range(reach_slabs + 1)]
    )
    doc_begin = query_index - positions
    distance = query_index[:, None] - key_index[None, :]
    visible = (distance >= 0) & (distance < window) & (key_index[None, :] >= doc_begin[:, None])
    scores = contract(query_rot, key_all)
    capped = soft_cap * jnp.tanh(scores / soft_cap)
    exp_scores = jnp.where(visible, jnp.exp(capped), 0.0)
    row_total = jnp.sum(exp_scores, axis=1)
    attn_rows = (
        jnp.dot(exp_scores.astype(jnp.bfloat16), value_all, preferred_element_type=jnp.float32)
        / row_total[:, None]
    ).astype(jnp.bfloat16)
    row_delta = jnp.sum(out_grad.astype(jnp.float32) * attn_rows.astype(jnp.float32), axis=1)
    soft_probs = exp_scores / row_total[:, None]
    prob_grad = contract(out_grad, value_all)
    score_grad = soft_probs * (prob_grad - row_delta[:, None]) * (1.0 - (capped / soft_cap) ** 2)
    score_low = score_grad.astype(jnp.bfloat16)
    probs_low = soft_probs.astype(jnp.bfloat16)
    rot_grad = jnp.dot(score_low, key_all, preferred_element_type=jnp.float32)
    query_grad = (rotate(rot_grad, cos_table, -sin_table) * query_scale).astype(jnp.bfloat16)
    key_grads = contract_rows(score_low, query_rot)
    value_grads = contract_rows(probs_low, out_grad)
    key_total = key_grads[:tok_rows]
    value_total = value_grads[:tok_rows]
    for offset in range(1, reach_slabs + 1):
        piece = jnp.concatenate(
            [
                key_grads[offset * tok_rows : (offset + 1) * tok_rows].astype(jnp.bfloat16),
                value_grads[offset * tok_rows : (offset + 1) * tok_rows].astype(jnp.bfloat16),
            ],
            axis=1,
        )
        recv = shifted(piece, "seq", -offset).astype(jnp.float32)
        key_total = key_total + recv[:, :HD]
        value_total = value_total + recv[:, HD:]
    outbound = jnp.where(is_even, value_total, key_total)
    partner_grad = from_partner(outbound.astype(jnp.bfloat16), "wt", 0).astype(outbound.dtype)
    pair_total = jnp.where(is_even, key_total, value_total) + partner_grad
    pair_grad = jnp.where(is_even, rotate(pair_total, cos_table, -sin_table), pair_total).astype(
        jnp.bfloat16
    )
    contribution = contract(w_query, query_grad) + contract(w_pair, pair_grad)
    row_part = jnp.sum(contribution * gained_full.T, axis=0)
    row_top = lax.reduce_precision(row_part, exponent_bits=8, mantissa_bits=7)
    row_hi = row_top.astype(jnp.bfloat16)
    row_lo = (row_part - row_top).astype(jnp.bfloat16)
    pad_rows = 16
    extra_rows = jnp.concatenate(
        [row_hi[None], row_lo[None], jnp.zeros((pad_rows - 2, tok_rows), jnp.bfloat16)], axis=0
    )
    packed = jnp.concatenate(
        [
            contribution.astype(jnp.bfloat16).reshape(groups, feat, tok_rows),
            jnp.broadcast_to(extra_rows[None], (groups, pad_rows, tok_rows)),
        ],
        axis=1,
    ).reshape(groups * (feat + pad_rows), tok_rows)
    scattered = jnp.sum(
        lax.all_to_all(
            packed.reshape(groups, feat + pad_rows, tok_rows),
            "wt",
            split_axis=0,
            concat_axis=0,
            tiled=True,
        ).astype(jnp.float32),
        axis=0,
    )
    normed_grad = scattered[:feat].astype(jnp.float32).T
    row_dots = scattered[feat].astype(jnp.float32) + scattered[feat + 1].astype(jnp.float32)
    scaled_grad = normed_grad * norm_gain[None, :]
    tokens_grad = (inv_rms[:, None] * (scaled_grad - scaled * (row_dots / D)[:, None])).astype(
        jnp.bfloat16
    )
    gain_part = jnp.sum(normed_grad * scaled, axis=0)
    grad_query = contract_rows(normed, query_grad)
    grad_pair = contract_rows(normed, pair_grad)
    grad_table = jnp.concatenate(
        [
            grad_query.reshape(row_blocks, BLK, BLK),
            grad_pair.reshape(row_blocks, BLK, BLK),
            jnp.zeros((1, BLK, BLK), jnp.float32),
        ],
        axis=0,
    )
    slot_grads = grad_table[arrival].reshape(groups, CAP, BLK, BLK)
    empty_block = jnp.zeros((1, BLK, BLK), jnp.bfloat16)
    returned = lax.all_to_all(
        slot_grads.astype(jnp.bfloat16), "wt", split_axis=0, concat_axis=0, tiled=True
    )
    owned_grads = jnp.concatenate([returned.reshape(-1, BLK, BLK), empty_block], axis=0)[slot_dest]
    n_seq = lax.axis_size("seq")
    slots = owned_grads.shape[0]
    chunk = slots * BLK * BLK // n_seq
    gain_width = -(-feat // 128) * 128
    reduced = lax.psum_scatter(owned_grads, "seq", scatter_dimension=0, tiled=True)
    gain_row = jnp.pad(gain_part.astype(jnp.bfloat16), (0, gain_width - feat))
    gathered_back = lax.all_gather(
        jnp.concatenate([reduced.reshape(1, chunk), gain_row[None]], axis=1),
        "seq",
        axis=0,
        tiled=True,
    )
    block_grads = gathered_back[:, :chunk].reshape(slots, BLK, BLK)
    gain_total = jnp.sum(gathered_back[:, chunk : chunk + feat].astype(jnp.float32), axis=0)
    return (attn_rows, tokens_grad, gain_total, block_grads[None])


def solution(mesh):
    placed = (
        P("seq", "wt"),
        P("wt"),
        P("seq"),
        P("wt", None, None, None),
        P("wt", None),
        P("seq", "wt"),
    )
    return jax.shard_map(
        body,
        mesh=mesh,
        in_specs=placed,
        out_specs=(P("seq", "wt"), P("seq", "wt"), P("wt"), P("wt", None, None, None)),
        check_vma=False,
    )
```

profile of v0, /device:TPU:1, one launch (start us, length us, event | category | flops | bytes accessed | tf_op | source)
XLA Modules:
  0.0 543.6 jit_solution(120040908919249098)
XLA Ops:
  11.1 11.2 %all-to-all-start = ((bf16[32,1,2]{2,1,0:T(2,128)(2,1)}), bf16[32,1,2]{2,1,0:T(2,128)(2,1)S(1)}, u32[]{:S(2)}, u32[]{:S(2)}) async-start(bf16[32,1,2]{2,1,0:T(2,128)(2,1)} %all_to_all.20), calls=%async_computation | async-start | bytes 32768 | tf_op jit(solution)/shard_map/all_to_all | solution.py:97
  22.8 6.7 %scatter_fusion = bf16[65,128,128]{2,1,0:T(8,128)(2,1)S(1)} fusion(bf16[65,128,128]{2,1,0:T(8,128)(2,1)S(1)} %broadcast_in_dim.31, s32[64]{0:T(128)S(1)} %fusion.54, bf16[64,128,128]{2,1,0:T(8,128)(2,1)} %bitcast.120), kind=kCustom, calls=%fused_computation.3 | custom fusion | bytes 6291712 | tf_op jit(solution)/shard_map/scatter | solution.py:82
  31.6 9.3 %all-to-all-start.1 = ((bf16[32,2,128,128]{3,2,1,0:T(8,128)(2,1)}), bf16[32,2,128,128]{3,2,1,0:T(8,128)(2,1)S(1)}, u32[]{:S(2)}, u32[]{:S(2)}) async-start(bf16[32,2,128,128]{3,2,1,0:T(8,128)(2,1)} %bitcast.115), calls=%async_computation.1 | async-start | bytes 4194304 | tf_op jit(solution)/shard_map/all_to_all | solution.py:90
  42.5 51.9 %all-to-all-done.1 = bf16[32,2,128,128]{3,2,1,0:T(8,128)(2,1)S(1)} async-done(((bf16[32,2,128,128]{3,2,1,0:T(8,128)(2,1)}), bf16[32,2,128,128]{3,2,1,0:T(8,128)(2,1)S(1)}, u32[]{:S(2)}, u32[]{:S(2)}) %all-to-all-start.1) | async-done | bytes 2097184 | tf_op jit(solution)/shard_map/all_to_all | solution.py:90
  96.4 6.7 %scatter_fusion.1 = bf16[73,128,128]{2,1,0:T(8,128)(2,1)S(1)} fusion(bf16[73,128,128]{2,1,0:T(8,128)(2,1)S(1)} %broadcast_in_dim.28, s32[64]{0:T(128)S(1)} %fusion.55, bf16[64,128,128]{2,1,0:T(8,128)(2,1)} %bitcast.114), kind=kCustom, calls=%fused_computation.4 | custom fusion | bytes 6291712 | tf_op jit(solution)/shard_map/scatter | solution.py:134
  104.6 16.9 %all-gather.4.cloned.1.call-done = bf16[232,4608]{0,1:T(8,128)(2,1)} async-done(((bf16[232,144]{0,1:T(8,128)(2,1)}), bf16[232,4608]{0,1:T(8,128)(2,1)}) %all-gather.4.cloned.1.call-update) | async-done | bytes 2138128 | tf_op jit(solution)/shard_map/all_gather | solution.py:111
  121.5 2.8 copy.23
  135.9 7.7 %collective-permute-start.8 = (bf16[224,256]{1,0:T(8,128)(2,1)S(1)}, bf16[224,256]{1,0:T(8,128)(2,1)S(1)}, u32[]{:S(2)}, u32[]{:S(2)}) collective-permute-start(bf16[224,256]{1,0:T(8,128)(2,1)S(1)} %pad_maximum_fusion.1), channel_id=1, source_target_pairs={{0,256},{32,288},{64,320},{96,352},{128,384},{160,416},{192,448},{... | collective-permute-start | bytes 344072 | tf_op jit(solution)/shard_map/ppermute | solution.py:28
  152.8 13.5 %collective-permute-done.2 = bf16[224,256]{1,0:T(8,128)(2,1)S(1)} collective-permute-done((bf16[224,256]{1,0:T(8,128)(2,1)S(1)}, bf16[224,256]{1,0:T(8,128)(2,1)S(1)}, u32[]{:S(2)}, u32[]{:S(2)}) %collective-permute-start.2) | collective-permute-done | bytes 114720 | tf_op jit(solution)/shard_map/ppermute | solution.py:28
  166.3 7.9 %collective-permute-start.3 = (bf16[224,256]{1,0:T(8,128)(2,1)S(1)}, bf16[224,256]{1,0:T(8,128)(2,1)S(1)}, u32[]{:S(2)}, u32[]{:S(2)}) collective-permute-start(bf16[224,256]{1,0:T(8,128)(2,1)S(1)} %pad_maximum_fusion.1), channel_id=1, source_target_pairs={{0,96},{32,128},{64,160},{96,192},{128,224},{160,256},{192,288},{2... | collective-permute-start | bytes 344072 | tf_op jit(solution)/shard_map/ppermute | solution.py:28
  176.3 6.8 %collective-permute-start.4 = (bf16[224,256]{1,0:T(8,128)(2,1)S(1)}, bf16[224,256]{1,0:T(8,128)(2,1)S(1)}, u32[]{:S(2)}, u32[]{:S(2)}) collective-permute-start(bf16[224,256]{1,0:T(8,128)(2,1)S(1)} %pad_maximum_fusion.1), channel_id=1, source_target_pairs={{0,128},{32,160},{64,192},{96,224},{128,256},{160,288},{192,320},{... | collective-permute-start | bytes 344072 | tf_op jit(solution)/shard_map/ppermute | solution.py:28
  200.6 9.9 %collective-permute-done.12 = bf16[224,256]{1,0:T(8,128)(2,1)S(1)} collective-permute-done((bf16[224,256]{1,0:T(8,128)(2,1)S(1)}, bf16[224,256]{1,0:T(8,128)(2,1)S(1)}, u32[]{:S(2)}, u32[]{:S(2)}) %collective-permute-start.12) | collective-permute-done | bytes 114720 | tf_op jit(solution)/shard_map/ppermute | solution.py:28
  212.5 7.4 %collective-permute-done.14 = bf16[224,256]{1,0:T(8,128)(2,1)S(1)} collective-permute-done((bf16[224,256]{1,0:T(8,128)(2,1)S(1)}, bf16[224,256]{1,0:T(8,128)(2,1)S(1)}, u32[]{:S(2)}, u32[]{:S(2)}) %collective-permute-start.14) | collective-permute-done | bytes 114720 | tf_op jit(solution)/shard_map/ppermute | solution.py:28
  220.2 10.2 %collective-permute-start.17 = (bf16[224,128]{1,0:T(8,128)(2,1)S(1)}, bf16[224,128]{1,0:T(8,128)(2,1)S(1)}, u32[]{:S(2)}, u32[]{:S(2)}) collective-permute-start(bf16[224,128]{1,0:T(8,128)(2,1)S(1)} %get-tuple-element.4), channel_id=1, source_target_pairs={{0,1},{1,0},{2,3},{3,2},{4,5},{5,4},{6,7},{7,6},{8,9},{9,8},{10,11... | collective-permute-start | bytes 172040 | tf_op jit(solution)/shard_map/ppermute | solution.py:22
  234.7 3.8 gather_fusion
  238.5 6.9 %all-to-all-start.3 = ((bf16[32,2,128,128]{3,2,1,0:T(8,128)(2,1)}), bf16[32,2,128,128]{3,2,1,0:T(8,128)(2,1)}, u32[]{:S(2)}, u32[]{:S(2)}) async-start(bf16[32,2,128,128]{3,2,1,0:T(8,128)(2,1)} %bitcast.116), calls=%async_computation.3 | async-start | bytes 4194304 | tf_op jit(solution)/shard_map/all_to_all | solution.py:249
  249.3 2.8 copy.21
  254.2 34.9 %all-to-all-done.3 = bf16[32,2,128,128]{3,2,1,0:T(8,128)(2,1)} async-done(((bf16[32,2,128,128]{3,2,1,0:T(8,128)(2,1)}), bf16[32,2,128,128]{3,2,1,0:T(8,128)(2,1)}, u32[]{:S(2)}, u32[]{:S(2)}) %all-to-all-start.3) | async-done | bytes 2097184 | tf_op jit(solution)/shard_map/all_to_all | solution.py:249
  289.1 12.7 %all-to-all-start.2 = ((bf16[32,160,224]{2,1,0:T(8,128)(2,1)}), bf16[32,160,224]{2,1,0:T(8,128)(2,1)S(1)}, u32[]{:S(2)}, u32[]{:S(2)}) async-start(bf16[32,160,224]{2,1,0:T(8,128)(2,1)} %pad_maximum_fusion), calls=%async_computation.2 | async-start | bytes 5242880 | tf_op jit(solution)/shard_map/all_to_all | solution.py:221
  301.8 3.2 concatenate.87
  305.1 3.7 gather_fusion.1
  308.9 63.8 %all-to-all-done.2 = bf16[32,160,224]{2,1,0:T(8,128)(2,1)S(1)} async-done(((bf16[32,160,224]{2,1,0:T(8,128)(2,1)}), bf16[32,160,224]{2,1,0:T(8,128)(2,1)S(1)}, u32[]{:S(2)}, u32[]{:S(2)}) %all-to-all-start.2) | async-done | bytes 2293792 | tf_op jit(solution)/shard_map/all_to_all | solution.py:221
  374.0 46.3 %reduce-scatter.2.cloned.1.call-done = bf16[4,128,128]{2,1,0:T(8,128)(2,1)} async-done(((bf16[64,128,128]{2,1,0:T(8,128)(2,1)}), bf16[4,128,128]{2,1,0:T(8,128)(2,1)}) %reduce-scatter.2.cloned.1.call-update) | async-done | bytes 131088 | tf_op jit(solution)/shard_map/reduce_scatter | solution.py:257
  422.2 109.8 %all-gather.6.cloned.1.call-done = bf16[16,1,65792]{2,1,0:T(2,128)(2,1)} async-done(((bf16[1,1,65792]{2,1,0:T(2,128)(2,1)}), bf16[16,1,65792]{2,1,0:T(2,128)(2,1)}) %all-gather.6.cloned.1.call-update) | async-done | bytes 2105360 | tf_op jit(solution)/shard_map/all_gather | solution.py:259
  (157 shorter events, 72.2 us)
Async XLA Ops:
  11.1 20.5 %all-to-all-start = ((bf16[32,1,2]{2,1,0:T(2,128)(2,1)}), bf16[32,1,2]{2,1,0:T(2,128)(2,1)S(1)}, u32[]{:S(2)}, u32[]{:S(2)}) async-start(bf16[32,1,2]{2,1,0:T(2,128)(2,1)} %all_to_all.20), calls=%async_computation | async-start | bytes 32768 | tf_op jit(solution)/shard_map/all_to_all | solution.py:97
  31.6 62.9 %all-to-all-start.1 = ((bf16[32,2,128,128]{3,2,1,0:T(8,128)(2,1)}), bf16[32,2,128,128]{3,2,1,0:T(8,128)(2,1)S(1)}, u32[]{:S(2)}, u32[]{:S(2)}) async-start(bf16[32,2,128,128]{3,2,1,0:T(8,128)(2,1)} %bitcast.115), calls=%async_computation.1 | async-start | bytes 4194304 | tf_op jit(solution)/shard_map/all_to_all | solution.py:90
  40.9 80.6 %all-gather.4.cloned.1.call-start = ((), (), s32[]{:S(2)}) async-start(), calls=%async_computation.5 | async-start | bytes 2433024 | tf_op jit(solution)/shard_map/all_gather | solution.py:111
  133.3 16.8 %collective-permute-start.1 = (bf16[224,256]{1,0:T(8,128)(2,1)S(1)}, bf16[224,256]{1,0:T(8,128)(2,1)S(1)}, u32[]{:S(2)}, u32[]{:S(2)}) collective-permute-start(bf16[224,256]{1,0:T(8,128)(2,1)S(1)} %pad_maximum_fusion.1), channel_id=1, source_target_pairs={{0,32},{32,64},{64,96},{96,128},{128,160},{160,192},{192,224},{224... | collective-permute-start | bytes 344072 | tf_op jit(solution)/shard_map/ppermute | solution.py:28
  135.9 48.8 %collective-permute-start.8 = (bf16[224,256]{1,0:T(8,128)(2,1)S(1)}, bf16[224,256]{1,0:T(8,128)(2,1)S(1)}, u32[]{:S(2)}, u32[]{:S(2)}) collective-permute-start(bf16[224,256]{1,0:T(8,128)(2,1)S(1)} %pad_maximum_fusion.1), channel_id=1, source_target_pairs={{0,256},{32,288},{64,320},{96,352},{128,384},{160,416},{192,448},{... | collective-permute-start | bytes 344072 | tf_op jit(solution)/shard_map/ppermute | solution.py:28
  143.7 41.0 %collective-permute-start.7 = (bf16[224,256]{1,0:T(8,128)(2,1)S(1)}, bf16[224,256]{1,0:T(8,128)(2,1)S(1)}, u32[]{:S(2)}, u32[]{:S(2)}) collective-permute-start(bf16[224,256]{1,0:T(8,128)(2,1)S(1)} %pad_maximum_fusion.1), channel_id=1, source_target_pairs={{0,224},{32,256},{64,288},{96,320},{128,352},{160,384},{192,416},{... | collective-permute-start | bytes 344072 | tf_op jit(solution)/shard_map/ppermute | solution.py:28
  146.1 38.6 %collective-permute-start.6 = (bf16[224,256]{1,0:T(8,128)(2,1)S(1)}, bf16[224,256]{1,0:T(8,128)(2,1)S(1)}, u32[]{:S(2)}, u32[]{:S(2)}) collective-permute-start(bf16[224,256]{1,0:T(8,128)(2,1)S(1)} %pad_maximum_fusion.1), channel_id=1, source_target_pairs={{0,192},{32,224},{64,256},{96,288},{128,320},{160,352},{192,384},{... | collective-permute-start | bytes 344072 | tf_op jit(solution)/shard_map/ppermute | solution.py:28
  148.9 35.8 %collective-permute-start.5 = (bf16[224,256]{1,0:T(8,128)(2,1)S(1)}, bf16[224,256]{1,0:T(8,128)(2,1)S(1)}, u32[]{:S(2)}, u32[]{:S(2)}) collective-permute-start(bf16[224,256]{1,0:T(8,128)(2,1)S(1)} %pad_maximum_fusion.1), channel_id=1, source_target_pairs={{0,160},{32,192},{64,224},{96,256},{128,288},{160,320},{192,352},{... | collective-permute-start | bytes 344072 | tf_op jit(solution)/shard_map/ppermute | solution.py:28
  150.2 16.1 %collective-permute-start.2 = (bf16[224,256]{1,0:T(8,128)(2,1)S(1)}, bf16[224,256]{1,0:T(8,128)(2,1)S(1)}, u32[]{:S(2)}, u32[]{:S(2)}) collective-permute-start(bf16[224,256]{1,0:T(8,128)(2,1)S(1)} %pad_maximum_fusion.1), channel_id=1, source_target_pairs={{0,64},{32,96},{64,128},{96,160},{128,192},{160,224},{192,256},{22... | collective-permute-start | bytes 344072 | tf_op jit(solution)/shard_map/ppermute | solution.py:28
  166.3 10.0 %collective-permute-start.3 = (bf16[224,256]{1,0:T(8,128)(2,1)S(1)}, bf16[224,256]{1,0:T(8,128)(2,1)S(1)}, u32[]{:S(2)}, u32[]{:S(2)}) collective-permute-start(bf16[224,256]{1,0:T(8,128)(2,1)S(1)} %pad_maximum_fusion.1), channel_id=1, source_target_pairs={{0,96},{32,128},{64,160},{96,192},{128,224},{160,256},{192,288},{2... | collective-permute-start | bytes 344072 | tf_op jit(solution)/shard_map/ppermute | solution.py:28
  176.3 8.3 %collective-permute-start.4 = (bf16[224,256]{1,0:T(8,128)(2,1)S(1)}, bf16[224,256]{1,0:T(8,128)(2,1)S(1)}, u32[]{:S(2)}, u32[]{:S(2)}) collective-permute-start(bf16[224,256]{1,0:T(8,128)(2,1)S(1)} %pad_maximum_fusion.1), channel_id=1, source_target_pairs={{0,128},{32,160},{64,192},{96,224},{128,256},{160,288},{192,320},{... | collective-permute-start | bytes 344072 | tf_op jit(solution)/shard_map/ppermute | solution.py:28
  190.4 6.8 %collective-permute-start.10 = (bf16[224,256]{1,0:T(8,128)(2,1)S(1)}, bf16[224,256]{1,0:T(8,128)(2,1)S(1)}, u32[]{:S(2)}, u32[]{:S(2)}) collective-permute-start(bf16[224,256]{1,0:T(8,128)(2,1)S(1)} %pad_maximum_fusion.3), channel_id=1, source_target_pairs={{64,0},{96,32},{128,64},{160,96},{192,128},{224,160},{256,192},{28... | collective-permute-start | bytes 344072 | tf_op jit(solution)/shard_map/ppermute | solution.py:28
  191.7 7.6 %collective-permute-start.11 = (bf16[224,256]{1,0:T(8,128)(2,1)S(1)}, bf16[224,256]{1,0:T(8,128)(2,1)S(1)}, u32[]{:S(2)}, u32[]{:S(2)}) collective-permute-start(bf16[224,256]{1,0:T(8,128)(2,1)S(1)} %pad_maximum_fusion.4), channel_id=1, source_target_pairs={{96,0},{128,32},{160,64},{192,96},{224,128},{256,160},{288,192},{3... | collective-permute-start | bytes 344072 | tf_op jit(solution)/shard_map/ppermute | solution.py:28
  193.1 17.5 %collective-permute-start.12 = (bf16[224,256]{1,0:T(8,128)(2,1)S(1)}, bf16[224,256]{1,0:T(8,128)(2,1)S(1)}, u32[]{:S(2)}, u32[]{:S(2)}) collective-permute-start(bf16[224,256]{1,0:T(8,128)(2,1)S(1)} %pad_maximum_fusion.5), channel_id=1, source_target_pairs={{128,0},{160,32},{192,64},{224,96},{256,128},{288,160},{320,192},{... | collective-permute-start | bytes 344072 | tf_op jit(solution)/shard_map/ppermute | solution.py:28
  194.4 18.1 %collective-permute-start.13 = (bf16[224,256]{1,0:T(8,128)(2,1)S(1)}, bf16[224,256]{1,0:T(8,128)(2,1)S(1)}, u32[]{:S(2)}, u32[]{:S(2)}) collective-permute-start(bf16[224,256]{1,0:T(8,128)(2,1)S(1)} %pad_maximum_fusion.6), channel_id=1, source_target_pairs={{160,0},{192,32},{224,64},{256,96},{288,128},{320,160},{352,192},{... | collective-permute-start | bytes 344072 | tf_op jit(solution)/shard_map/ppermute | solution.py:28
  195.7 24.2 %collective-permute-start.14 = (bf16[224,256]{1,0:T(8,128)(2,1)S(1)}, bf16[224,256]{1,0:T(8,128)(2,1)S(1)}, u32[]{:S(2)}, u32[]{:S(2)}) collective-permute-start(bf16[224,256]{1,0:T(8,128)(2,1)S(1)} %pad_maximum_fusion.7), channel_id=1, source_target_pairs={{192,0},{224,32},{256,64},{288,96},{320,128},{352,160},{384,192},{... | collective-permute-start | bytes 344072 | tf_op jit(solution)/shard_map/ppermute | solution.py:28
  197.3 22.7 %collective-permute-start.15 = (bf16[224,256]{1,0:T(8,128)(2,1)S(1)}, bf16[224,256]{1,0:T(8,128)(2,1)S(1)}, u32[]{:S(2)}, u32[]{:S(2)}) collective-permute-start(bf16[224,256]{1,0:T(8,128)(2,1)S(1)} %pad_maximum_fusion.8), channel_id=1, source_target_pairs={{224,0},{256,32},{288,64},{320,96},{352,128},{384,160},{416,192},{... | collective-permute-start | bytes 344072 | tf_op jit(solution)/shard_map/ppermute | solution.py:28
  199.4 20.7 %collective-permute-start.16 = (bf16[224,256]{1,0:T(8,128)(2,1)S(1)}, bf16[224,256]{1,0:T(8,128)(2,1)S(1)}, u32[]{:S(2)}, u32[]{:S(2)}) collective-permute-start(bf16[224,256]{1,0:T(8,128)(2,1)S(1)} %pad_maximum_fusion.9), channel_id=1, source_target_pairs={{256,0},{288,32},{320,64},{352,96},{384,128},{416,160},{448,192},{... | collective-permute-start | bytes 344072 | tf_op jit(solution)/shard_map/ppermute | solution.py:28
  210.5 9.5 %collective-permute-start.9 = (bf16[224,256]{1,0:T(8,128)(2,1)S(1)}, bf16[224,256]{1,0:T(8,128)(2,1)S(1)}, u32[]{:S(2)}, u32[]{:S(2)}) collective-permute-start(bf16[224,256]{1,0:T(8,128)(2,1)S(1)} %pad_maximum_fusion.2), channel_id=1, source_target_pairs={{32,0},{64,32},{96,64},{128,96},{160,128},{192,160},{224,192},{256... | collective-permute-start | bytes 344072 | tf_op jit(solution)/shard_map/ppermute | solution.py:28
  220.2 11.2 %collective-permute-start.17 = (bf16[224,128]{1,0:T(8,128)(2,1)S(1)}, bf16[224,128]{1,0:T(8,128)(2,1)S(1)}, u32[]{:S(2)}, u32[]{:S(2)}) collective-permute-start(bf16[224,128]{1,0:T(8,128)(2,1)S(1)} %get-tuple-element.4), channel_id=1, source_target_pairs={{0,1},{1,0},{2,3},{3,2},{4,5},{5,4},{6,7},{7,6},{8,9},{9,8},{10,11... | collective-permute-start | bytes 172040 | tf_op jit(solution)/shard_map/ppermute | solution.py:22
  238.5 50.6 %all-to-all-start.3 = ((bf16[32,2,128,128]{3,2,1,0:T(8,128)(2,1)}), bf16[32,2,128,128]{3,2,1,0:T(8,128)(2,1)}, u32[]{:S(2)}, u32[]{:S(2)}) async-start(bf16[32,2,128,128]{3,2,1,0:T(8,128)(2,1)} %bitcast.116), calls=%async_computation.3 | async-start | bytes 4194304 | tf_op jit(solution)/shard_map/all_to_all | solution.py:249
  289.1 83.6 %all-to-all-start.2 = ((bf16[32,160,224]{2,1,0:T(8,128)(2,1)}), bf16[32,160,224]{2,1,0:T(8,128)(2,1)S(1)}, u32[]{:S(2)}, u32[]{:S(2)}) async-start(bf16[32,160,224]{2,1,0:T(8,128)(2,1)} %pad_maximum_fusion), calls=%async_computation.2 | async-start | bytes 5242880 | tf_op jit(solution)/shard_map/all_to_all | solution.py:221
  301.8 118.5 %reduce-scatter.2.cloned.1.call-start = ((), (), s32[]{:S(2)}) async-start(), calls=%async_computation.6 | async-start | bytes 2228224 | tf_op jit(solution)/shard_map/reduce_scatter | solution.py:257
  308.8 223.2 %all-gather.6.cloned.1.call-start = ((), (), s32[]{:S(2)}) async-start(), calls=%async_computation.7 | async-start | bytes 4473856 | tf_op jit(solution)/shard_map/all_gather | solution.py:259
  (9 other events, 42.4 us)
Sparse Core Ops, SparseCore 0:
  45.4 76.0 all-gather.3
  308.9 111.2 reduce-scatter.1
  422.9 109.0 all-gather.5
where the time goes:
time: 545 us; the launch traced here: 544 us
  waiting for transfers between devices  360 us (66%)
  starting transfers between devices  96.4 us (18%)
  local copies, waits for them, and re-layouts  44.3 us (8%)
  other arithmetic  16.3 us (3%)
  between operations  14.6 us (3%)
  matrix products  12.2 us (2%)
    all_gather x1, waiting for transfers between devices, body(): lax.all_gather(jnp.concatenate([reduced.reshape(1, chunk), gain_row[None]...  110 us
    all_to_all x1, waiting for transfers between devices, body(): lax.all_to_all(packed.reshape(groups, feat + pad_rows, tok_rows), 'wt', s...  63.8 us
    all_to_all x1, waiting for transfers between devices, body(): lax.all_to_all(outgoing[:dump_slot].reshape(groups, CAP, BLK, BLK), 'wt',...  51.9 us
    reduce_scatter x1, waiting for transfers between devices, body(): lax.psum_scatter(owned_grads, 'seq', scatter_dimension=0, tiled=True)  46.3 us
    ppermute x16, starting transfers between devices, shifted(): lax.ppermute(value, axis, [(source, source + steps) for source in range(i...  43.7 us
    ppermute x16, waiting for transfers between devices, shifted(): lax.ppermute(value, axis, [(source, source + steps) for source in range(i...  35.4 us
    all_to_all x1, waiting for transfers between devices, body(): lax.all_to_all(slot_grads.astype(jnp.bfloat16), 'wt', split_axis=0, conca...  34.9 us
    all_gather x1, waiting for transfers between devices, body(): lax.all_gather(jnp.concatenate([tokens_in, gain_rows, jnp.zeros((side_row...  16.9 us
  transfers between devices with their start and end apart: 25, of which 15 were waited for; matrix products, arithmetic and copies ran while one was open for 7% of the time, Pallas kernels for 0%

commit v1 on v0

--- a/solution.py
+++ b/solution.py
@@ -108,13 +108,22 @@
     gain_lo = gain_rest - gain_mid
     gain_rows = jnp.stack([gain_hi, gain_mid, gain_lo]).astype(jnp.bfloat16)
     side_rows = 8
-    gathered = lax.all_gather(
-        jnp.concatenate(
-            [tokens_in, gain_rows, jnp.zeros((side_rows - 3, feat), jnp.bfloat16)], axis=0
+    gathered = jnp.concatenate(
+        lax.all_to_all(
+            jnp.stack(
+                [
+                    jnp.concatenate(
+                        [tokens_in, gain_rows, jnp.zeros((side_rows - 3, feat), jnp.bfloat16)],
+                        axis=0,
+                    )
+                ]
+                * lax.axis_size("wt")
+            ),
+            "wt",
+            0,
+            0,
         ),
-        "wt",
         axis=1,
-        tiled=True,
     )
     tokens_full = gathered[:tok_rows]
     gain_parts = gathered[tok_rows : tok_rows + 3].astype(jnp.float32)

time: 545 us -> 580 us (1.064)
  waiting for transfers between devices: 360 us -> 394 us
  starting transfers between devices: 96.4 us -> 79.5 us
  local copies, waits for them, and re-layouts: 44.3 us -> 56.6 us
    all_to_all x0 -> x1, waiting for transfers between devices: none -> 38.5 us  [body(): lax.all_to_all(jnp.stack([jnp.concatenate([tokens_in, gain_rows, jnp.zero...]
    all_gather x1 -> x0, waiting for transfers between devices: 16.9 us -> none  [body(): lax.all_gather(jnp.concatenate([tokens_in, gain_rows, jnp.zeros((side_row...]
    ppermute x16, waiting for transfers between devices: 35.4 us -> 45.3 us  [shifted(): lax.ppermute(value, axis, [(source, source + steps) for source in range(i...]
    all_to_all x1, starting transfers between devices: 12.7 us -> 4.47 us  [body(): lax.all_to_all(packed.reshape(groups, feat + pad_rows, tok_rows), 'wt', s...]
    all_to_all x1, waiting for transfers between devices: 34.9 us -> 42.2 us  [body(): lax.all_to_all(slot_grads.astype(jnp.bfloat16), 'wt', split_axis=0, conca...]
    ppermute x2, starting transfers between devices: 12.4 us -> 5.29 us  [from_partner(): return lax.ppermute(block, axis, route)]
    convert_element_type x0 -> x1, local copies, waits for them, and re-layouts: none -> 5.84 us  [body(): full_f32 = tokens_full.astype(jnp.float32)]
  transfers between devices with their start and end apart: 25 -> 25, of which waited for: 15 -> 13; matrix products, arithmetic and copies ran while one was open for 7% -> 9% of each run, Pallas kernels for 0% -> 0%
where the time goes in v1:
time: 580 us; the launch traced here: 578 us
  waiting for transfers between devices  394 us (68%)
  starting transfers between devices  79.5 us (14%)
  local copies, waits for them, and re-layouts  56.6 us (10%)
  other arithmetic  21 us (4%)
  between operations  15.1 us (3%)
  matrix products  12.1 us (2%)
    all_gather x1, waiting for transfers between devices, body(): lax.all_gather(jnp.concatenate([reduced.reshape(1, chunk), gain_row[None]...  107 us
    all_to_all x1, waiting for transfers between devices, body(): lax.all_to_all(packed.reshape(groups, feat + pad_rows, tok_rows), 'wt', s...  66.8 us
    all_to_all x1, waiting for transfers between devices, body(): lax.all_to_all(outgoing[:dump_slot].reshape(groups, CAP, BLK, BLK), 'wt',...  51.3 us
    ppermute x16, waiting for transfers between devices, shifted(): lax.ppermute(value, axis, [(source, source + steps) for source in range(i...  45.3 us
    reduce_scatter x1, waiting for transfers between devices, body(): lax.psum_scatter(owned_grads, 'seq', scatter_dimension=0, tiled=True)  42.3 us
    all_to_all x1, waiting for transfers between devices, body(): lax.all_to_all(slot_grads.astype(jnp.bfloat16), 'wt', split_axis=0, conca...  42.2 us
    ppermute x16, starting transfers between devices, shifted(): lax.ppermute(value, axis, [(source, source + steps) for source in range(i...  39 us
    all_to_all x1, waiting for transfers between devices, body(): lax.all_to_all(jnp.stack([jnp.concatenate([tokens_in, gain_rows, jnp.zero...  38.5 us
  transfers between devices with their start and end apart: 25, of which 13 were waited for; matrix products, arithmetic and copies ran while one was open for 9% of the time, Pallas kernels for 0%

profile of v1, /device:TPU:1, one launch (start us, length us, event | category | flops | bytes accessed | tf_op | source)
XLA Modules:
  0.0 578.2 jit_solution(24463076736338705)
XLA Ops:
  11.1 11.2 %all-to-all-start.1 = ((bf16[32,1,2]{2,1,0:T(2,128)(2,1)}), bf16[32,1,2]{2,1,0:T(2,128)(2,1)S(1)}, u32[]{:S(2)}, u32[]{:S(2)}) async-start(bf16[32,1,2]{2,1,0:T(2,128)(2,1)} %all_to_all.24), calls=%async_computation.1 | async-start | bytes 32768 | tf_op jit(solution)/shard_map/all_to_all | solution.py:97
  22.8 6.7 %scatter_fusion = bf16[65,128,128]{2,1,0:T(8,128)(2,1)S(1)} fusion(bf16[65,128,128]{2,1,0:T(8,128)(2,1)S(1)} %broadcast_in_dim.31, s32[64]{0:T(128)S(1)} %fusion.59, bf16[64,128,128]{2,1,0:T(8,128)(2,1)} %bitcast.138), kind=kCustom, calls=%fused_computation.3 | custom fusion | bytes 6291712 | tf_op jit(solution)/shard_map/scatter | solution.py:82
  31.6 9.2 %all-to-all-start.2 = ((bf16[32,2,128,128]{3,2,1,0:T(8,128)(2,1)}), bf16[32,2,128,128]{3,2,1,0:T(8,128)(2,1)S(1)}, u32[]{:S(2)}, u32[]{:S(2)}) async-start(bf16[32,2,128,128]{3,2,1,0:T(8,128)(2,1)} %bitcast.137), calls=%async_computation.2 | async-start | bytes 4194304 | tf_op jit(solution)/shard_map/all_to_all | solution.py:90
  41.3 51.3 %all-to-all-done.2 = bf16[32,2,128,128]{3,2,1,0:T(8,128)(2,1)S(1)} async-done(((bf16[32,2,128,128]{3,2,1,0:T(8,128)(2,1)}), bf16[32,2,128,128]{3,2,1,0:T(8,128)(2,1)S(1)}, u32[]{:S(2)}, u32[]{:S(2)}) %all-to-all-start.2) | async-done | bytes 2097184 | tf_op jit(solution)/shard_map/all_to_all | solution.py:90
  94.7 5.3 all-to-all-start
  105.6 10.1 %scatter_fusion.1 = bf16[73,128,128]{2,1,0:T(8,128)(2,1)} fusion(bf16[73,128,128]{2,1,0:T(8,128)(2,1)} %broadcast_in_dim.28, s32[64]{0:T(128)S(1)} %fusion.60, bf16[64,128,128]{2,1,0:T(8,128)(2,1)} %bitcast.136), kind=kCustom, calls=%fused_computation.4 | custom fusion | bytes 6291712 | tf_op jit(solution)/shard_map/scatter | solution.py:143
  118.5 38.5 %all-to-all-done = bf16[32,232,144]{1,2,0:T(8,128)(2,1)S(1)} async-done(((bf16[32,232,144]{1,2,0:T(8,128)(2,1)}), bf16[32,232,144]{1,2,0:T(8,128)(2,1)S(1)}, u32[]{:S(2)}, u32[]{:S(2)}) %all-to-all-start) | async-done | bytes 2138144 | tf_op jit(solution)/shard_map/all_to_all | solution.py:112
  171.6 5.8 %copy.57 = f32[224,4608]{1,0:T(8,128)} copy(f32[224,4608]{0,1:T(8,128)} %bitcast.128) | data formatting | bytes 8257536 | tf_op jit(solution)/shard_map/convert_element_type | solution.py:131
  177.6 4.6 collective-permute-start.2
  182.2 7.0 %collective-permute-start.3 = (bf16[224,256]{1,0:T(8,128)(2,1)S(1)}, bf16[224,256]{1,0:T(8,128)(2,1)S(1)}, u32[]{:S(2)}, u32[]{:S(2)}) collective-permute-start(bf16[224,256]{1,0:T(8,128)(2,1)S(1)} %pad_maximum_fusion.1), channel_id=1, source_target_pairs={{0,96},{32,128},{64,160},{96,192},{128,224},{160,256},{192,288},{2... | collective-permute-start | bytes 344072 | tf_op jit(solution)/shard_map/ppermute | solution.py:28
  189.2 6.1 %collective-permute-start.4 = (bf16[224,256]{1,0:T(8,128)(2,1)S(1)}, bf16[224,256]{1,0:T(8,128)(2,1)S(1)}, u32[]{:S(2)}, u32[]{:S(2)}) collective-permute-start(bf16[224,256]{1,0:T(8,128)(2,1)S(1)} %pad_maximum_fusion.1), channel_id=1, source_target_pairs={{0,128},{32,160},{64,192},{96,224},{128,256},{160,288},{192,320},{... | collective-permute-start | bytes 344072 | tf_op jit(solution)/shard_map/ppermute | solution.py:28
  195.3 3.7 collective-permute-start.5
  205.0 10.1 %collective-permute-done.6 = bf16[224,256]{1,0:T(8,128)(2,1)S(1)} collective-permute-done((bf16[224,256]{1,0:T(8,128)(2,1)S(1)}, bf16[224,256]{1,0:T(8,128)(2,1)S(1)}, u32[]{:S(2)}, u32[]{:S(2)}) %collective-permute-start.6) | collective-permute-done | bytes 114720 | tf_op jit(solution)/shard_map/ppermute | solution.py:28
  239.0 16.9 %collective-permute-done.12 = bf16[224,256]{1,0:T(8,128)(2,1)S(1)} collective-permute-done((bf16[224,256]{1,0:T(8,128)(2,1)S(1)}, bf16[224,256]{1,0:T(8,128)(2,1)S(1)}, u32[]{:S(2)}, u32[]{:S(2)}) %collective-permute-start.12) | collective-permute-done | bytes 114720 | tf_op jit(solution)/shard_map/ppermute | solution.py:28
  255.9 11.6 %collective-permute-done.14 = bf16[224,256]{1,0:T(8,128)(2,1)S(1)} collective-permute-done((bf16[224,256]{1,0:T(8,128)(2,1)S(1)}, bf16[224,256]{1,0:T(8,128)(2,1)S(1)}, u32[]{:S(2)}, u32[]{:S(2)}) %collective-permute-start.14) | collective-permute-done | bytes 114720 | tf_op jit(solution)/shard_map/ppermute | solution.py:28
  274.9 3.8 gather_fusion
  278.7 4.8 all-to-all-start.4
  293.4 42.2 %all-to-all-done.4 = bf16[32,2,128,128]{3,2,1,0:T(8,128)(2,1)} async-done(((bf16[32,2,128,128]{3,2,1,0:T(8,128)(2,1)}), bf16[32,2,128,128]{3,2,1,0:T(8,128)(2,1)}, u32[]{:S(2)}, u32[]{:S(2)}) %all-to-all-start.4) | async-done | bytes 2097184 | tf_op jit(solution)/shard_map/all_to_all | solution.py:258
  335.6 4.5 all-to-all-start.3
  340.1 3.2 concatenate.87
  343.4 3.7 gather_fusion.1
  347.2 66.8 %all-to-all-done.3 = bf16[32,160,224]{2,1,0:T(8,128)(2,1)S(1)} async-done(((bf16[32,160,224]{2,1,0:T(8,128)(2,1)}), bf16[32,160,224]{2,1,0:T(8,128)(2,1)S(1)}, u32[]{:S(2)}, u32[]{:S(2)}) %all-to-all-start.3) | async-done | bytes 2293792 | tf_op jit(solution)/shard_map/all_to_all | solution.py:230
  415.2 42.3 %reduce-scatter.2.cloned.1.call-done = bf16[4,128,128]{2,1,0:T(8,128)(2,1)} async-done(((bf16[64,128,128]{2,1,0:T(8,128)(2,1)}), bf16[4,128,128]{2,1,0:T(8,128)(2,1)}) %reduce-scatter.2.cloned.1.call-update) | async-done | bytes 131088 | tf_op jit(solution)/shard_map/reduce_scatter | solution.py:266
  459.5 106.7 %all-gather.3.cloned.1.call-done = bf16[16,1,65792]{2,1,0:T(2,128)(2,1)} async-done(((bf16[1,1,65792]{2,1,0:T(2,128)(2,1)}), bf16[16,1,65792]{2,1,0:T(2,128)(2,1)}) %all-gather.3.cloned.1.call-update) | async-done | bytes 2105360 | tf_op jit(solution)/shard_map/all_gather | solution.py:268
  (190 shorter events, 86.8 us)
Async XLA Ops:
  11.1 20.5 %all-to-all-start.1 = ((bf16[32,1,2]{2,1,0:T(2,128)(2,1)}), bf16[32,1,2]{2,1,0:T(2,128)(2,1)S(1)}, u32[]{:S(2)}, u32[]{:S(2)}) async-start(bf16[32,1,2]{2,1,0:T(2,128)(2,1)} %all_to_all.24), calls=%async_computation.1 | async-start | bytes 32768 | tf_op jit(solution)/shard_map/all_to_all | solution.py:97
  31.6 61.0 %all-to-all-start.2 = ((bf16[32,2,128,128]{3,2,1,0:T(8,128)(2,1)}), bf16[32,2,128,128]{3,2,1,0:T(8,128)(2,1)S(1)}, u32[]{:S(2)}, u32[]{:S(2)}) async-start(bf16[32,2,128,128]{3,2,1,0:T(8,128)(2,1)} %bitcast.137), calls=%async_computation.2 | async-start | bytes 4194304 | tf_op jit(solution)/shard_map/all_to_all | solution.py:90
  94.7 62.3 %all-to-all-start = ((bf16[32,232,144]{1,2,0:T(8,128)(2,1)}), bf16[32,232,144]{1,2,0:T(8,128)(2,1)S(1)}, u32[]{:S(2)}, u32[]{:S(2)}) async-start(bf16[32,232,144]{1,2,0:T(8,128)(2,1)} %stack.15), calls=%async_computation | async-start | bytes 4718592 | tf_op jit(solution)/shard_map/all_to_all | solution.py:112
  169.5 29.6 %collective-permute-start.1 = (bf16[224,256]{1,0:T(8,128)(2,1)S(1)}, bf16[224,256]{1,0:T(8,128)(2,1)S(1)}, u32[]{:S(2)}, u32[]{:S(2)}) collective-permute-start(bf16[224,256]{1,0:T(8,128)(2,1)S(1)} %pad_maximum_fusion.1), channel_id=1, source_target_pairs={{0,32},{32,64},{64,96},{96,128},{128,160},{160,192},{192,224},{224... | collective-permute-start | bytes 344072 | tf_op jit(solution)/shard_map/ppermute | solution.py:28
  177.6 23.5 %collective-permute-start.2 = (bf16[224,256]{1,0:T(8,128)(2,1)S(1)}, bf16[224,256]{1,0:T(8,128)(2,1)S(1)}, u32[]{:S(2)}, u32[]{:S(2)}) collective-permute-start(bf16[224,256]{1,0:T(8,128)(2,1)S(1)} %pad_maximum_fusion.1), channel_id=1, source_target_pairs={{0,64},{32,96},{64,128},{96,160},{128,192},{160,224},{192,256},{22... | collective-permute-start | bytes 344072 | tf_op jit(solution)/shard_map/ppermute | solution.py:28
  182.2 20.8 %collective-permute-start.3 = (bf16[224,256]{1,0:T(8,128)(2,1)S(1)}, bf16[224,256]{1,0:T(8,128)(2,1)S(1)}, u32[]{:S(2)}, u32[]{:S(2)}) collective-permute-start(bf16[224,256]{1,0:T(8,128)(2,1)S(1)} %pad_maximum_fusion.1), channel_id=1, source_target_pairs={{0,96},{32,128},{64,160},{96,192},{128,224},{160,256},{192,288},{2... | collective-permute-start | bytes 344072 | tf_op jit(solution)/shard_map/ppermute | solution.py:28
  189.2 15.8 %collective-permute-start.4 = (bf16[224,256]{1,0:T(8,128)(2,1)S(1)}, bf16[224,256]{1,0:T(8,128)(2,1)S(1)}, u32[]{:S(2)}, u32[]{:S(2)}) collective-permute-start(bf16[224,256]{1,0:T(8,128)(2,1)S(1)} %pad_maximum_fusion.1), channel_id=1, source_target_pairs={{0,128},{32,160},{64,192},{96,224},{128,256},{160,288},{192,320},{... | collective-permute-start | bytes 344072 | tf_op jit(solution)/shard_map/ppermute | solution.py:28
  195.3 9.7 %collective-permute-start.5 = (bf16[224,256]{1,0:T(8,128)(2,1)S(1)}, bf16[224,256]{1,0:T(8,128)(2,1)S(1)}, u32[]{:S(2)}, u32[]{:S(2)}) collective-permute-start(bf16[224,256]{1,0:T(8,128)(2,1)S(1)} %pad_maximum_fusion.1), channel_id=1, source_target_pairs={{0,160},{32,192},{64,224},{96,256},{128,288},{160,320},{192,352},{... | collective-permute-start | bytes 344072 | tf_op jit(solution)/shard_map/ppermute | solution.py:28
  199.1 16.0 %collective-permute-start.6 = (bf16[224,256]{1,0:T(8,128)(2,1)S(1)}, bf16[224,256]{1,0:T(8,128)(2,1)S(1)}, u32[]{:S(2)}, u32[]{:S(2)}) collective-permute-start(bf16[224,256]{1,0:T(8,128)(2,1)S(1)} %pad_maximum_fusion.1), channel_id=1, source_target_pairs={{0,192},{32,224},{64,256},{96,288},{128,320},{160,352},{192,384},{... | collective-permute-start | bytes 344072 | tf_op jit(solution)/shard_map/ppermute | solution.py:28
  201.1 14.1 %collective-permute-start.7 = (bf16[224,256]{1,0:T(8,128)(2,1)S(1)}, bf16[224,256]{1,0:T(8,128)(2,1)S(1)}, u32[]{:S(2)}, u32[]{:S(2)}) collective-permute-start(bf16[224,256]{1,0:T(8,128)(2,1)S(1)} %pad_maximum_fusion.1), channel_id=1, source_target_pairs={{0,224},{32,256},{64,288},{96,320},{128,352},{160,384},{192,416},{... | collective-permute-start | bytes 344072 | tf_op jit(solution)/shard_map/ppermute | solution.py:28
  203.0 14.6 %collective-permute-start.8 = (bf16[224,256]{1,0:T(8,128)(2,1)S(1)}, bf16[224,256]{1,0:T(8,128)(2,1)S(1)}, u32[]{:S(2)}, u32[]{:S(2)}) collective-permute-start(bf16[224,256]{1,0:T(8,128)(2,1)S(1)} %pad_maximum_fusion.1), channel_id=1, source_target_pairs={{0,256},{32,288},{64,320},{96,352},{128,384},{160,416},{192,448},{... | collective-permute-start | bytes 344072 | tf_op jit(solution)/shard_map/ppermute | solution.py:28
  223.4 6.7 %collective-permute-start.9 = (bf16[224,256]{1,0:T(8,128)(2,1)S(1)}, bf16[224,256]{1,0:T(8,128)(2,1)S(1)}, u32[]{:S(2)}, u32[]{:S(2)}) collective-permute-start(bf16[224,256]{1,0:T(8,128)(2,1)S(1)} %pad_maximum_fusion.2), channel_id=1, source_target_pairs={{32,0},{64,32},{96,64},{128,96},{160,128},{192,160},{224,192},{256... | collective-permute-start | bytes 344072 | tf_op jit(solution)/shard_map/ppermute | solution.py:28
  224.7 9.7 %collective-permute-start.10 = (bf16[224,256]{1,0:T(8,128)(2,1)S(1)}, bf16[224,256]{1,0:T(8,128)(2,1)S(1)}, u32[]{:S(2)}, u32[]{:S(2)}) collective-permute-start(bf16[224,256]{1,0:T(8,128)(2,1)S(1)} %pad_maximum_fusion.3), channel_id=1, source_target_pairs={{64,0},{96,32},{128,64},{160,96},{192,128},{224,160},{256,192},{28... | collective-permute-start | bytes 344072 | tf_op jit(solution)/shard_map/ppermute | solution.py:28
  226.0 11.0 %collective-permute-start.11 = (bf16[224,256]{1,0:T(8,128)(2,1)S(1)}, bf16[224,256]{1,0:T(8,128)(2,1)S(1)}, u32[]{:S(2)}, u32[]{:S(2)}) collective-permute-start(bf16[224,256]{1,0:T(8,128)(2,1)S(1)} %pad_maximum_fusion.4), channel_id=1, source_target_pairs={{96,0},{128,32},{160,64},{192,96},{224,128},{256,160},{288,192},{3... | collective-permute-start | bytes 344072 | tf_op jit(solution)/shard_map/ppermute | solution.py:28
  227.3 28.5 %collective-permute-start.12 = (bf16[224,256]{1,0:T(8,128)(2,1)S(1)}, bf16[224,256]{1,0:T(8,128)(2,1)S(1)}, u32[]{:S(2)}, u32[]{:S(2)}) collective-permute-start(bf16[224,256]{1,0:T(8,128)(2,1)S(1)} %pad_maximum_fusion.5), channel_id=1, source_target_pairs={{128,0},{160,32},{192,64},{224,96},{256,128},{288,160},{320,192},{... | collective-permute-start | bytes 344072 | tf_op jit(solution)/shard_map/ppermute | solution.py:28
  228.7 27.2 %collective-permute-start.13 = (bf16[224,256]{1,0:T(8,128)(2,1)S(1)}, bf16[224,256]{1,0:T(8,128)(2,1)S(1)}, u32[]{:S(2)}, u32[]{:S(2)}) collective-permute-start(bf16[224,256]{1,0:T(8,128)(2,1)S(1)} %pad_maximum_fusion.6), channel_id=1, source_target_pairs={{160,0},{192,32},{224,64},{256,96},{288,128},{320,160},{352,192},{... | collective-permute-start | bytes 344072 | tf_op jit(solution)/shard_map/ppermute | solution.py:28
  230.1 37.4 %collective-permute-start.14 = (bf16[224,256]{1,0:T(8,128)(2,1)S(1)}, bf16[224,256]{1,0:T(8,128)(2,1)S(1)}, u32[]{:S(2)}, u32[]{:S(2)}) collective-permute-start(bf16[224,256]{1,0:T(8,128)(2,1)S(1)} %pad_maximum_fusion.7), channel_id=1, source_target_pairs={{192,0},{224,32},{256,64},{288,96},{320,128},{352,160},{384,192},{... | collective-permute-start | bytes 344072 | tf_op jit(solution)/shard_map/ppermute | solution.py:28
  234.4 33.1 %collective-permute-start.15 = (bf16[224,256]{1,0:T(8,128)(2,1)S(1)}, bf16[224,256]{1,0:T(8,128)(2,1)S(1)}, u32[]{:S(2)}, u32[]{:S(2)}) collective-permute-start(bf16[224,256]{1,0:T(8,128)(2,1)S(1)} %pad_maximum_fusion.8), channel_id=1, source_target_pairs={{224,0},{256,32},{288,64},{320,96},{352,128},{384,160},{416,192},{... | collective-permute-start | bytes 344072 | tf_op jit(solution)/shard_map/ppermute | solution.py:28
  237.0 30.6 %collective-permute-start.16 = (bf16[224,256]{1,0:T(8,128)(2,1)S(1)}, bf16[224,256]{1,0:T(8,128)(2,1)S(1)}, u32[]{:S(2)}, u32[]{:S(2)}) collective-permute-start(bf16[224,256]{1,0:T(8,128)(2,1)S(1)} %pad_maximum_fusion.9), channel_id=1, source_target_pairs={{256,0},{288,32},{320,64},{352,96},{384,128},{416,160},{448,192},{... | collective-permute-start | bytes 344072 | tf_op jit(solution)/shard_map/ppermute | solution.py:28
  267.7 3.9 collective-permute-start.17
  278.7 56.8 %all-to-all-start.4 = ((bf16[32,2,128,128]{3,2,1,0:T(8,128)(2,1)}), bf16[32,2,128,128]{3,2,1,0:T(8,128)(2,1)}, u32[]{:S(2)}, u32[]{:S(2)}) async-start(bf16[32,2,128,128]{3,2,1,0:T(8,128)(2,1)} %bitcast.24), calls=%async_computation.4 | async-start | bytes 4194304 | tf_op jit(solution)/shard_map/all_to_all | solution.py:258
  335.6 78.4 %all-to-all-start.3 = ((bf16[32,160,224]{2,1,0:T(8,128)(2,1)}), bf16[32,160,224]{2,1,0:T(8,128)(2,1)S(1)}, u32[]{:S(2)}, u32[]{:S(2)}) async-start(bf16[32,160,224]{2,1,0:T(8,128)(2,1)} %pad_maximum_fusion), calls=%async_computation.3 | async-start | bytes 5242880 | tf_op jit(solution)/shard_map/all_to_all | solution.py:230
  340.1 117.5 %reduce-scatter.2.cloned.1.call-start = ((), (), s32[]{:S(2)}) async-start(), calls=%async_computation.6 | async-start | bytes 2228224 | tf_op jit(solution)/shard_map/reduce_scatter | solution.py:266
  347.1 219.1 %all-gather.3.cloned.1.call-start = ((), (), s32[]{:S(2)}) async-start(), calls=%async_computation.7 | async-start | bytes 4473856 | tf_op jit(solution)/shard_map/all_gather | solution.py:268
  (24 other events, 399.0 us)
Sparse Core Ops, SparseCore 0:
  347.2 110.2 reduce-scatter.1
  460.2 105.9 all-gather.2
